TPU v7x, 32 devices: a whole 2x2x4 slice. The times are simulated.
32 devices in a mesh: groups: 2 (over y), tm: 4 (over x, core), width: 4 (over z).
Axes of the slice: x: 2, y: 2, z: 4, core: 2. Of those that a mesh axis runs over, the one named last changes fastest.
Arguments:
- video: bfloat16 [32, 12, 48, 256], P(('groups', 'tm'), None, 'width'), parts along dimension 0, may hold values from -6 to 6
- conv_w: bfloat16 [2, 3, 3, 256, 256], replicated, may hold values from -0.125 to 0.125
- depth_k: float32 [2, 16, 256], replicated, may hold values from -1.5 to 1.5
- proj_w: bfloat16 [2, 256, 256], replicated, may hold values from -0.375 to 0.375
Outputs:
- result: bfloat16 [32, 12, 48, 256], P(('groups', 'tm'), None, 'width'), parts along dimension 0
There are 2 independent parts, one for each index of `groups`. A program takes and returns all parts, laid end to end along the dimension named above; an argument that names none is the same for every part. Nothing has to cross between parts.
All inputs are finite; a program needn't handle non-finite values.
Results may differ from a plain program's by a relative error of at most 0.0058.
Values may be sent and summed in bfloat16 or wider, within the bound.
No kernel may reach another device: no remote copies, remote signals or barrier semaphores. Data moves between devices by JAX's collectives and lax.ppermute only.
A program may use at most 64 MiB of HBM per device.

v0:
```python
import jax
import jax.numpy as jnp
from jax import lax
from jax.sharding import PartitionSpec as P

BLOCKS = 2


def conv3x3(x, weight):
    return lax.conv_general_dilated(
        x,
        weight,
        window_strides=(1, 1),
        padding="VALID",
        dimension_numbers=("NHWC", "HWIO", "NHWC"),
        preferred_element_type=jnp.float32,
    )


def block(x, weight, kernel, proj):
    chans = x.shape[-1]
    hidden = jax.nn.silu(conv3x3(x, weight)).astype(jnp.bfloat16)
    frames = hidden.shape[0]
    values = hidden.astype(jnp.float32)
    depth = values * kernel[0]
    for lag in range(1, frames):
        shifted = jnp.pad(values[: frames - lag], ((lag, 0), (0, 0), (0, 0), (0, 0)))
        depth = depth + shifted * kernel[lag]
    depth = depth.astype(jnp.bfloat16)
    mixed = jnp.dot(depth.reshape(-1, chans), proj, preferred_element_type=jnp.float32)
    mixed = mixed.reshape(hidden.shape).astype(jnp.bfloat16)
    inner = x[:, 1:-1, 1:-1, :]
    return (inner.astype(jnp.float32) + mixed.astype(jnp.float32)).astype(jnp.bfloat16)


def shards(video, conv_w, depth_k, proj_w):
    bands = lax.axis_size("tm")
    sides = lax.axis_size("width")
    band = lax.axis_index("tm")
    side = lax.axis_index("width")
    frames, height, cols, chans = video.shape
    rows = height // bands
    halo = BLOCKS
    padded = jnp.pad(video, ((0, 0), (halo, halo), (0, 0), (0, 0)))
    pieces = jnp.stack([padded[:, r * rows : r * rows + rows + 2 * halo] for r in range(bands)])
    gathered = lax.all_to_all(pieces, "tm", 0, 0, tiled=False)
    gathered = gathered.reshape(bands * frames, rows + 2 * halo, cols, chans)
    up = [(i, i + 1) for i in range(sides - 1)]
    down = [(i + 1, i) for i in range(sides - 1)]
    before = lax.ppermute(gathered[:, :, cols - halo :], "width", up)
    after = lax.ppermute(gathered[:, :, :halo], "width", down)
    inner = block(gathered, conv_w[0], depth_k[0], proj_w[0])
    reach = 2 * halo
    rims = jnp.concatenate(
        [before, gathered[:, :, :reach], gathered[:, :, cols - reach :], after], axis=2
    )
    rims = block(rims, conv_w[0], depth_k[0], proj_w[0])
    state = jnp.concatenate([rims[:, :, :halo], inner, rims[:, :, rims.shape[2] - halo :]], axis=2)
    for b in range(1, BLOCKS):
        left = halo - b
        n_rows, n_cols = (state.shape[1], state.shape[2])
        row = band * rows - left + lax.broadcasted_iota(jnp.int32, (n_rows, n_cols), 0)
        col = side * cols - left + lax.broadcasted_iota(jnp.int32, (n_rows, n_cols), 1)
        inside = (row >= 0) & (row < height) & (col >= 0) & (col < sides * cols)
        state = jnp.where(inside[None, :, :, None], state, jnp.zeros((), state.dtype))
        state = block(state, conv_w[b], depth_k[b], proj_w[b])
    return lax.all_to_all(state, "tm", 0, 1, tiled=True)


def solution(mesh):
    return jax.shard_map(
        shards,
        mesh=mesh,
        in_specs=(P(("groups", "tm"), None, "width", None), P(), P(), P()),
        out_specs=P(("groups", "tm"), None, "width", None),
        check_vma=False,
    )
```

profile of v0, /device:TPU:0, one launch (start us, length us, event | category | flops | bytes accessed | tf_op | source)
XLA Modules:
  0.0 48.9 jit_solution(6434809782838823936)
XLA Ops:
  0.0 0.0 copy-start
  0.0 1.4 %fusion.38 = (bf16[1,4,7,12,256]{4,1,3,2,0:T(4,128)(2,1)S(1)}, bf16[1,4,7,12,256]{4,1,3,2,0:T(4,128)(2,1)S(1)}, bf16[1,4,7,12,256]{4,1,3,2,0:T(4,128)(2,1)S(1)}, bf16[1,4,7,12,256]{4,1,3,2,0:T(4,128)(2,1)S(1)}) fusion(bf16[4,12,12,256]{3,0,2,1:T(4,128)(2,1)} %param.4), kind=kLoop, calls=%fused_computation.40 | loop fusion | bytes 1327104 | tf_op jit(solution)/shard_map/stack | solution.py:45
  1.4 1.5 %pad_maximum_fusion = bf16[4,4,7,12,256]{4,1,3,2,0:T(4,128)(2,1)} fusion(bf16[1,4,7,12,256]{4,1,3,2,0:T(4,128)(2,1)S(1)} %get-tuple-element.12, bf16[1,4,7,12,256]{4,1,3,2,0:T(4,128)(2,1)S(1)} %get-tuple-element.13, bf16[1,4,7,12,256]{4,1,3,2,0:T(4,128)(2,1)S(1)} %get-tuple-element.14, bf16[1,4,7,12,256]{4,1,3,2,0:T(4,128)(2,1)S(1)} %get-tuple-element.11), kind=kLoop, calls=%fused_computation.26 | loop fusion | flops 1032192 | bytes 1376256 | tf_op jit(solution)/shard_map/stack | solution.py:45
  2.8 4.2 %all-to-all-start = ((bf16[4,4,7,12,256]{4,1,3,2,0:T(4,128)(2,1)}), bf16[4,4,7,12,256]{4,1,3,2,0:T(4,128)(2,1)S(1)}, u32[]{:S(2)}, u32[]{:S(2)}) async-start(bf16[4,4,7,12,256]{4,1,3,2,0:T(4,128)(2,1)} %pad_maximum_fusion), calls=%async_computation | async-start | bytes 1376256 | tf_op jit(solution)/shard_map/all_to_all | solution.py:46
  7.1 0.1 and_and_fusion
  7.2 0.0 copy-done
  7.2 10.4 %all-to-all-done = bf16[4,4,7,12,256]{4,1,3,2,0:T(4,128)(2,1)S(1)} async-done(((bf16[4,4,7,12,256]{4,1,3,2,0:T(4,128)(2,1)}), bf16[4,4,7,12,256]{4,1,3,2,0:T(4,128)(2,1)S(1)}, u32[]{:S(2)}, u32[]{:S(2)}) %all-to-all-start) | async-done | bytes 688160 | tf_op jit(solution)/shard_map/all_to_all | solution.py:46
  17.7 0.3 copy.7
  17.9 0.2 reshape.154
  18.1 2.4 %fusion.18 = f32[16,5,10,256]{3,0,2,1:T(8,128)S(1)} fusion(bf16[16,7,12,256]{3,0,2,1:T(8,128)(2,1)S(1)} %reshape.154, bf16[2,3,3,256,256]{4,3,2,1,0:T(8,128)(2,1)} %param.5), kind=kOutput, calls=%fused_computation.21 | convolution fusion | flops 944947200 | bytes 2686976 | tf_op jit(solution)/shard_map/conv_general_dilated | solution.py:10
  20.5 0.0 copy-start.2
  20.8 4.2 %collective-permute-start = (bf16[16,7,2,256]{3,0,2,1:T(8,128)(2,1)S(1)}, bf16[16,7,2,256]{3,0,2,1:T(8,128)(2,1)S(1)}, u32[]{:S(2)}, u32[]{:S(2)}) collective-permute-start(bf16[16,7,2,256]{3,0,2,1:T(8,128)(2,1)S(1)} %get-tuple-element.5), channel_id=1, source_target_pairs={{0,1},{1,2},{2,3},{4,5},{5,6},{6,7},{8,9},{9,10},{10,11},{12,13},{... | collective-permute-start | bytes 344072 | tf_op jit(solution)/shard_map/ppermute | solution.py:50
  25.0 1.3 %collective-permute-start.1 = (bf16[16,7,2,256]{3,0,2,1:T(8,128)(2,1)S(1)}, bf16[16,7,2,256]{3,0,2,1:T(8,128)(2,1)S(1)}, u32[]{:S(2)}, u32[]{:S(2)}) collective-permute-start(bf16[16,7,2,256]{3,0,2,1:T(8,128)(2,1)S(1)} %get-tuple-element.6), channel_id=1, source_target_pairs={{1,0},{2,1},{3,2},{5,4},{6,5},{7,6},{9,8},{10,9},{11,10},{13,12},{... | collective-permute-start | bytes 344072 | tf_op jit(solution)/shard_map/ppermute | solution.py:51
  26.3 0.0 copy-done.2
  26.3 0.0 copy-start.1
  26.3 2.0 %fusion.2 = bf16[16,5,10,256]{3,0,2,1:T(8,128)(2,1)S(1)} fusion(bf16[16,7,12,256]{3,0,2,1:T(8,128)(2,1)S(1)} %reshape.154, f32[1,5,10,256]{3,0,2,1:T(1,128)S(1)} %slice.498, f32[2,5,10,256]{3,0,2,1:T(2,128)S(1)} %slice.497, f32[3,5,10,256]{3,0,2,1:T(4,128)S(1)} %slice.496, f32[4,5,10,256]{3,0,2,1:T(4,128)S(1)} %slice.495, f32[5,5,10,256]{3,0,2,1:T(8,128)S(1)} %slice.494, ...), kind=kOutput, calls=%fused_computation.3 | convolution fusion | flops 112435200 | bytes 9721856 | tf_op jit(solution)/shard_map/dot_general | solution.py:30
  28.3 0.0 collective-permute-done
  28.3 3.4 %collective-permute-done.1 = bf16[16,7,2,256]{3,0,2,1:T(8,128)(2,1)S(1)} collective-permute-done((bf16[16,7,2,256]{3,0,2,1:T(8,128)(2,1)S(1)}, bf16[16,7,2,256]{3,0,2,1:T(8,128)(2,1)S(1)}, u32[]{:S(2)}, u32[]{:S(2)}) %collective-permute-start.1) | collective-permute-done | bytes 114720 | tf_op jit(solution)/shard_map/ppermute | solution.py:51
  31.7 0.0 copy-done.1
  31.7 1.1 %fusion.23 = f32[16,5,10,256]{3,0,2,1:T(8,128)S(1)} fusion(bf16[2,3,3,256,256]{4,3,2,1,0:T(8,128)(2,1)S(1)} %copy-done.1, bf16[16,7,2,256]{3,0,2,1:T(8,128)(2,1)S(1)} %collective-permute-done.1, bf16[16,7,4,256]{3,0,2,1:T(8,128)(2,1)S(1)} %get-tuple-element.8, bf16[16,7,4,256]{3,0,2,1:T(8,128)(2,1)S(1)} %get-tuple-element.7, ...), kind=kOutput, calls=%fused_computation.25 | convolution fusion | flops 945979392 | bytes 2686976 | tf_op jit(solution)/shard_map/conv_general_dilated | solution.py:10
  33.1 2.3 %add_convert_fusion.1 = bf16[16,5,10,256]{3,0,2,1:T(8,128)(2,1)S(1)} fusion(bf16[16,7,2,256]{3,0,2,1:T(8,128)(2,1)S(1)} %collective-permute-done.1, bf16[16,7,4,256]{3,0,2,1:T(8,128)(2,1)S(1)} %get-tuple-element.8, bf16[16,7,4,256]{3,0,2,1:T(8,128)(2,1)S(1)} %get-tuple-element.7, bf16[16,7,2,256]{3,0,2,1:T(8,128)(2,1)S(1)} %collective-permute-done, ...), kind=kOutput, calls=%fused_computation.22 | convolution fusion | flops 113049600 | bytes 10000384 | tf_op jit(solution)/shard_map/dot_general | solution.py:30
  35.5 0.1 maximum_select_fusion
  35.6 0.9 %fusion.35 = f32[16,3,12,256]{3,0,2,1:T(8,128)S(1)} fusion(bf16[16,5,14,256]{3,0,2,1:T(8,128)(2,1)S(1)} %maximum_select_fusion, bf16[2,3,3,256,256]{4,3,2,1,0:T(8,128)(2,1)S(1)} %copy-done.1), kind=kOutput, calls=%fused_computation.36 | convolution fusion | flops 680361984 | bytes 2342912 | tf_op jit(solution)/shard_map/conv_general_dilated | solution.py:10
  36.7 1.4 %fusion.6 = bf16[16,3,12,256]{3,0,2,1:T(8,128)(2,1)S(1)} fusion(bf16[16,5,14,256]{3,0,2,1:T(8,128)(2,1)S(1)} %maximum_select_fusion, f32[1,3,12,256]{3,0,2,1:T(1,128)S(1)} %slice.515, f32[2,3,12,256]{3,0,2,1:T(2,128)S(1)} %slice.514, f32[3,3,12,256]{3,0,2,1:T(4,128)S(1)} %slice.513, f32[4,3,12,256]{3,0,2,1:T(4,128)S(1)} %slice.512, ...), kind=kOutput, calls=%fused_computation.9 | convolution fusion | flops 80953344 | bytes 7041024 | tf_op jit(solution)/shard_map/dot_general | solution.py:30
  38.2 0.1 copy.8
  38.3 9.8 %all_to_all.23 = bf16[16,3,12,256]{3,2,1,0:T(8,128)(2,1)S(1)} all-to-all(bf16[16,3,12,256]{3,2,1,0:T(8,128)(2,1)S(1)} %copy.8), channel_id=1, replica_groups=mesh['groups'=2,'tm'=4,'width'=4] {'tm'}, dimensions={0} | all-to-all | bytes 589824 | tf_op jit(solution)/shard_map/all_to_all | solution.py:67
  48.1 0.9 %copy.9 = bf16[4,4,3,12,256]{4,0,3,2,1:T(4,128)(2,1)} copy(bf16[4,4,3,12,256]{4,3,2,0,1:T(8,128)(2,1)S(1)} %bitcast.126) | data formatting | bytes 589824 | tf_op jit(solution)/shard_map/all_to_all | solution.py:67
  (31 shorter events, 0.7 us)
Async XLA Ops:
  0.0 7.2 %copy-start = (f32[2,16,256]{2,1,0:T(8,128)S(1)}, f32[2,16,256]{2,1,0:T(8,128)}, u32[]{:S(2)}) copy-start(f32[2,16,256]{2,1,0:T(8,128)} %param.6) | copy-start | bytes 98308
  2.8 14.8 %all-to-all-start = ((bf16[4,4,7,12,256]{4,1,3,2,0:T(4,128)(2,1)}), bf16[4,4,7,12,256]{4,1,3,2,0:T(4,128)(2,1)S(1)}, u32[]{:S(2)}, u32[]{:S(2)}) async-start(bf16[4,4,7,12,256]{4,1,3,2,0:T(4,128)(2,1)} %pad_maximum_fusion), calls=%async_computation | async-start | bytes 1376256 | tf_op jit(solution)/shard_map/all_to_all | solution.py:46
  20.5 5.8 %copy-start.2 = (bf16[2,256,256]{2,1,0:T(8,128)(2,1)S(1)}, bf16[2,256,256]{2,1,0:T(8,128)(2,1)}, u32[]{:S(2)}) copy-start(bf16[2,256,256]{2,1,0:T(8,128)(2,1)} %param.7) | copy-start | bytes 786436
  20.8 7.5 %collective-permute-start = (bf16[16,7,2,256]{3,0,2,1:T(8,128)(2,1)S(1)}, bf16[16,7,2,256]{3,0,2,1:T(8,128)(2,1)S(1)}, u32[]{:S(2)}, u32[]{:S(2)}) collective-permute-start(bf16[16,7,2,256]{3,0,2,1:T(8,128)(2,1)S(1)} %get-tuple-element.5), channel_id=1, source_target_pairs={{0,1},{1,2},{2,3},{4,5},{5,6},{6,7},{8,9},{9,10},{10,11},{12,13},{... | collective-permute-start | bytes 344072 | tf_op jit(solution)/shard_map/ppermute | solution.py:50
  25.0 6.7 %collective-permute-start.1 = (bf16[16,7,2,256]{3,0,2,1:T(8,128)(2,1)S(1)}, bf16[16,7,2,256]{3,0,2,1:T(8,128)(2,1)S(1)}, u32[]{:S(2)}, u32[]{:S(2)}) collective-permute-start(bf16[16,7,2,256]{3,0,2,1:T(8,128)(2,1)S(1)} %get-tuple-element.6), channel_id=1, source_target_pairs={{1,0},{2,1},{3,2},{5,4},{6,5},{7,6},{9,8},{10,9},{11,10},{13,12},{... | collective-permute-start | bytes 344072 | tf_op jit(solution)/shard_map/ppermute | solution.py:51
  26.3 5.4 %copy-start.1 = (bf16[2,3,3,256,256]{4,3,2,1,0:T(8,128)(2,1)S(1)}, bf16[2,3,3,256,256]{4,3,2,1,0:T(8,128)(2,1)}, u32[]{:S(2)}) copy-start(bf16[2,3,3,256,256]{4,3,2,1,0:T(8,128)(2,1)} %param.5) | copy-start | bytes 7077892
where the time goes:
time: 49.2 us; the launch traced here: 48.9 us
  waiting for transfers between devices  13.8 us (28%)
  matrix products  10.1 us (21%)
  blocking collectives  9.8 us (20%)
  starting transfers between devices  9.71 us (20%)
  local copies, waits for them, and re-layouts  3.47 us (7%)
  other arithmetic  1.71 us (3%)
    all_to_all x1, waiting for transfers between devices, shards(): gathered = lax.all_to_all(pieces, 'tm', 0, 0, tiled=False)  10.4 us
    all_to_all x1, blocking collectives, shards(): return lax.all_to_all(state, 'tm', 0, 1, tiled=True)  9.8 us
    dot_general x3, matrix products, block(): jnp.dot(depth.reshape(-1, chans), proj, preferred_element_type=jnp.float32)  5.69 us
    conv_general_dilated x3, matrix products, conv3x3(): lax.conv_general_dilated(x, weight, window_strides=(1, 1), padding='VALID...  4.41 us
    all_to_all x1, starting transfers between devices, shards(): gathered = lax.all_to_all(pieces, 'tm', 0, 0, tiled=False)  4.24 us
    ppermute x1, starting transfers between devices, shards(): before = lax.ppermute(gathered[:, :, cols - halo:], 'width', up)  4.18 us
    ppermute x1, waiting for transfers between devices, shards(): after = lax.ppermute(gathered[:, :, :halo], 'width', down)  3.36 us
    another operation x1, other arithmetic, shards(): jnp.stack([padded[:, r * rows:r * rows + rows + 2 * halo] for r in range(...  1.47 us
  transfers between devices with their start and end apart: 3, of which 2 were waited for; matrix products, arithmetic and copies ran while one was open for 4% of the time, Pallas kernels for 0%

commit v1 on v0

--- a/solution.py
+++ b/solution.py
@@ -64,7 +64,15 @@
         inside = (row >= 0) & (row < height) & (col >= 0) & (col < sides * cols)
         state = jnp.where(inside[None, :, :, None], state, jnp.zeros((), state.dtype))
         state = block(state, conv_w[b], depth_k[b], proj_w[b])
-    return lax.all_to_all(state, "tm", 0, 1, tiled=True)
+    return jnp.concatenate(
+        lax.all_to_all(
+            jnp.stack(jnp.split(state, lax.psum(1, axis_name="tm"), axis=0), 0),
+            axis_name="tm",
+            split_axis=0,
+            concat_axis=0,
+        ),
+        axis=1,
+    )
 
 
 def solution(mesh):

time: 49.2 us -> 48.3 us (0.982)
  blocking collectives: 9.8 us -> 8.72 us
    all_to_all x1, blocking collectives: 9.8 us -> 8.72 us  [shards(): lax.all_to_all(jnp.stack(jnp.split(state, lax.psum(1, axis_name='tm'), ax...]
    all_to_all x1 -> x0, local copies, waits for them, and re-layouts: 0.87 us -> none  [shards(): return lax.all_to_all(state, 'tm', 0, 1, tiled=True)]
    unnamed x6 -> x7, local copies, waits for them, and re-layouts: 0.02 us -> 0.73 us
where the time goes in v1:
time: 48.3 us; the launch traced here: 48 us
  waiting for transfers between devices  13.8 us (29%)
  matrix products  10.1 us (21%)
  starting transfers between devices  9.72 us (20%)
  blocking collectives  8.72 us (18%)
  local copies, waits for them, and re-layouts  3.32 us (7%)
  other arithmetic  1.99 us (4%)
    all_to_all x1, waiting for transfers between devices, shards(): gathered = lax.all_to_all(pieces, 'tm', 0, 0, tiled=False)  10.4 us
    all_to_all x1, blocking collectives, shards(): lax.all_to_all(jnp.stack(jnp.split(state, lax.psum(1, axis_name='tm'), ax...  8.72 us
    dot_general x3, matrix products, block(): jnp.dot(depth.reshape(-1, chans), proj, preferred_element_type=jnp.float32)  5.69 us
    conv_general_dilated x3, matrix products, conv3x3(): lax.conv_general_dilated(x, weight, window_strides=(1, 1), padding='VALID...  4.41 us
    all_to_all x1, starting transfers between devices, shards(): gathered = lax.all_to_all(pieces, 'tm', 0, 0, tiled=False)  4.24 us
    ppermute x1, starting transfers between devices, shards(): before = lax.ppermute(gathered[:, :, cols - halo:], 'width', up)  4.19 us
    ppermute x1, waiting for transfers between devices, shards(): after = lax.ppermute(gathered[:, :, :halo], 'width', down)  3.36 us
    another operation x1, other arithmetic, shards(): jnp.stack([padded[:, r * rows:r * rows + rows + 2 * halo] for r in range(...  1.48 us
  transfers between devices with their start and end apart: 3, of which 2 were waited for; matrix products, arithmetic and copies ran while one was open for 4% of the time, Pallas kernels for 0%

profile of v1, /device:TPU:0, one launch (start us, length us, event | category | flops | bytes accessed | tf_op | source)
XLA Modules:
  0.0 48.0 jit_solution(4058733956180179016)
XLA Ops:
  0.0 0.0 copy-start
  0.0 1.4 %fusion.38 = (bf16[1,4,7,12,256]{4,1,3,2,0:T(4,128)(2,1)S(1)}, bf16[1,4,7,12,256]{4,1,3,2,0:T(4,128)(2,1)S(1)}, bf16[1,4,7,12,256]{4,1,3,2,0:T(4,128)(2,1)S(1)}, bf16[1,4,7,12,256]{4,1,3,2,0:T(4,128)(2,1)S(1)}) fusion(bf16[4,12,12,256]{3,0,2,1:T(4,128)(2,1)} %param.4), kind=kLoop, calls=%fused_computation.41 | loop fusion | bytes 1327104 | tf_op jit(solution)/shard_map/stack | solution.py:45
  1.4 1.5 %pad_maximum_fusion = bf16[4,4,7,12,256]{4,1,3,2,0:T(4,128)(2,1)} fusion(bf16[1,4,7,12,256]{4,1,3,2,0:T(4,128)(2,1)S(1)} %get-tuple-element.16, bf16[1,4,7,12,256]{4,1,3,2,0:T(4,128)(2,1)S(1)} %get-tuple-element.17, bf16[1,4,7,12,256]{4,1,3,2,0:T(4,128)(2,1)S(1)} %get-tuple-element.18, bf16[1,4,7,12,256]{4,1,3,2,0:T(4,128)(2,1)S(1)} %get-tuple-element.15), kind=kLoop, calls=%fused_computation.26 | loop fusion | flops 1032192 | bytes 1376256 | tf_op jit(solution)/shard_map/stack | solution.py:45
  2.9 4.2 %all-to-all-start = ((bf16[4,4,7,12,256]{4,1,3,2,0:T(4,128)(2,1)}), bf16[4,4,7,12,256]{4,1,3,2,0:T(4,128)(2,1)S(1)}, u32[]{:S(2)}, u32[]{:S(2)}) async-start(bf16[4,4,7,12,256]{4,1,3,2,0:T(4,128)(2,1)} %pad_maximum_fusion), calls=%async_computation | async-start | bytes 1376256 | tf_op jit(solution)/shard_map/all_to_all | solution.py:46
  7.1 0.1 and_and_fusion
  7.2 0.0 copy-done
  7.2 10.4 %all-to-all-done = bf16[4,4,7,12,256]{4,1,3,2,0:T(4,128)(2,1)S(1)} async-done(((bf16[4,4,7,12,256]{4,1,3,2,0:T(4,128)(2,1)}), bf16[4,4,7,12,256]{4,1,3,2,0:T(4,128)(2,1)S(1)}, u32[]{:S(2)}, u32[]{:S(2)}) %all-to-all-start) | async-done | bytes 688160 | tf_op jit(solution)/shard_map/all_to_all | solution.py:46
  17.7 0.3 copy.5
  17.9 0.2 reshape.160
  18.1 2.4 %fusion.18 = f32[16,5,10,256]{3,0,2,1:T(8,128)S(1)} fusion(bf16[16,7,12,256]{3,0,2,1:T(8,128)(2,1)S(1)} %reshape.160, bf16[2,3,3,256,256]{4,3,2,1,0:T(8,128)(2,1)} %param.5), kind=kOutput, calls=%fused_computation.21 | convolution fusion | flops 944947200 | bytes 2686976 | tf_op jit(solution)/shard_map/conv_general_dilated | solution.py:10
  20.5 0.0 copy-start.2
  20.8 4.2 %collective-permute-start = (bf16[16,7,2,256]{3,0,2,1:T(8,128)(2,1)S(1)}, bf16[16,7,2,256]{3,0,2,1:T(8,128)(2,1)S(1)}, u32[]{:S(2)}, u32[]{:S(2)}) collective-permute-start(bf16[16,7,2,256]{3,0,2,1:T(8,128)(2,1)S(1)} %get-tuple-element.5), channel_id=1, source_target_pairs={{0,1},{1,2},{2,3},{4,5},{5,6},{6,7},{8,9},{9,10},{10,11},{12,13},{... | collective-permute-start | bytes 344072 | tf_op jit(solution)/shard_map/ppermute | solution.py:50
  25.0 1.3 %collective-permute-start.1 = (bf16[16,7,2,256]{3,0,2,1:T(8,128)(2,1)S(1)}, bf16[16,7,2,256]{3,0,2,1:T(8,128)(2,1)S(1)}, u32[]{:S(2)}, u32[]{:S(2)}) collective-permute-start(bf16[16,7,2,256]{3,0,2,1:T(8,128)(2,1)S(1)} %get-tuple-element.6), channel_id=1, source_target_pairs={{1,0},{2,1},{3,2},{5,4},{6,5},{7,6},{9,8},{10,9},{11,10},{13,12},{... | collective-permute-start | bytes 344072 | tf_op jit(solution)/shard_map/ppermute | solution.py:51
  26.3 0.0 copy-done.2
  26.3 0.0 copy-start.1
  26.3 2.0 %fusion.2 = bf16[16,5,10,256]{3,0,2,1:T(8,128)(2,1)S(1)} fusion(bf16[16,7,12,256]{3,0,2,1:T(8,128)(2,1)S(1)} %reshape.160, f32[1,5,10,256]{3,0,2,1:T(1,128)S(1)} %slice.498, f32[2,5,10,256]{3,0,2,1:T(2,128)S(1)} %slice.497, f32[3,5,10,256]{3,0,2,1:T(4,128)S(1)} %slice.496, f32[4,5,10,256]{3,0,2,1:T(4,128)S(1)} %slice.495, f32[5,5,10,256]{3,0,2,1:T(8,128)S(1)} %slice.494, ...), kind=kOutput, calls=%fused_computation.3 | convolution fusion | flops 112435200 | bytes 9721856 | tf_op jit(solution)/shard_map/dot_general | solution.py:30
  28.3 0.0 collective-permute-done
  28.4 3.4 %collective-permute-done.1 = bf16[16,7,2,256]{3,0,2,1:T(8,128)(2,1)S(1)} collective-permute-done((bf16[16,7,2,256]{3,0,2,1:T(8,128)(2,1)S(1)}, bf16[16,7,2,256]{3,0,2,1:T(8,128)(2,1)S(1)}, u32[]{:S(2)}, u32[]{:S(2)}) %collective-permute-start.1) | collective-permute-done | bytes 114720 | tf_op jit(solution)/shard_map/ppermute | solution.py:51
  31.7 0.0 copy-done.1
  31.7 1.1 %fusion.23 = f32[16,5,10,256]{3,0,2,1:T(8,128)S(1)} fusion(bf16[2,3,3,256,256]{4,3,2,1,0:T(8,128)(2,1)S(1)} %copy-done.1, bf16[16,7,2,256]{3,0,2,1:T(8,128)(2,1)S(1)} %collective-permute-done.1, bf16[16,7,4,256]{3,0,2,1:T(8,128)(2,1)S(1)} %get-tuple-element.8, bf16[16,7,4,256]{3,0,2,1:T(8,128)(2,1)S(1)} %get-tuple-element.7, ...), kind=kOutput, calls=%fused_computation.25 | convolution fusion | flops 945979392 | bytes 2686976 | tf_op jit(solution)/shard_map/conv_general_dilated | solution.py:10
  33.1 2.3 %add_convert_fusion.1 = bf16[16,5,10,256]{3,0,2,1:T(8,128)(2,1)S(1)} fusion(bf16[16,7,2,256]{3,0,2,1:T(8,128)(2,1)S(1)} %collective-permute-done.1, bf16[16,7,4,256]{3,0,2,1:T(8,128)(2,1)S(1)} %get-tuple-element.8, bf16[16,7,4,256]{3,0,2,1:T(8,128)(2,1)S(1)} %get-tuple-element.7, bf16[16,7,2,256]{3,0,2,1:T(8,128)(2,1)S(1)} %collective-permute-done, ...), kind=kOutput, calls=%fused_computation.22 | convolution fusion | flops 113049600 | bytes 10000384 | tf_op jit(solution)/shard_map/dot_general | solution.py:30
  35.5 0.1 maximum_select_fusion
  35.6 0.9 %fusion.35 = f32[16,3,12,256]{3,0,2,1:T(8,128)S(1)} fusion(bf16[16,5,14,256]{3,0,2,1:T(8,128)(2,1)S(1)} %maximum_select_fusion, bf16[2,3,3,256,256]{4,3,2,1,0:T(8,128)(2,1)S(1)} %copy-done.1), kind=kOutput, calls=%fused_computation.36 | convolution fusion | flops 680361984 | bytes 2342912 | tf_op jit(solution)/shard_map/conv_general_dilated | solution.py:10
  36.8 1.4 %fusion.6 = bf16[16,3,12,256]{3,0,2,1:T(8,128)(2,1)S(1)} fusion(bf16[16,5,14,256]{3,0,2,1:T(8,128)(2,1)S(1)} %maximum_select_fusion, f32[1,3,12,256]{3,0,2,1:T(1,128)S(1)} %slice.515, f32[2,3,12,256]{3,0,2,1:T(2,128)S(1)} %slice.514, f32[3,3,12,256]{3,0,2,1:T(4,128)S(1)} %slice.513, f32[4,3,12,256]{3,0,2,1:T(4,128)S(1)} %slice.512, ...), kind=kOutput, calls=%fused_computation.9 | convolution fusion | flops 80953344 | bytes 7041024 | tf_op jit(solution)/shard_map/dot_general | solution.py:30
  38.2 0.1 slice_bitcast_fusion.5
  38.3 0.3 pad_maximum_fusion.1
  38.6 8.7 %all_to_all.10 = bf16[4,4,3,12,256]{4,1,3,2,0:T(4,128)(2,1)S(1)} all-to-all(bf16[4,4,3,12,256]{4,1,3,2,0:T(4,128)(2,1)S(1)} %pad_maximum_fusion.1), channel_id=1, replica_groups=mesh['groups'=2,'tm'=4,'width'=4] {'tm'}, dimensions={0} | all-to-all | bytes 589824 | tf_op jit(solution)/shard_map/all_to_all | solution.py:68
  47.3 0.7 %copy.9 = bf16[4,12,12,256]{3,0,2,1:T(4,128)(2,1)} copy(bf16[4,12,12,256]{3,0,2,1:T(4,128)(2,1)S(1)} %bitcast.133) | data formatting | bytes 589824
  (31 shorter events, 0.7 us)
Async XLA Ops:
  0.0 7.2 %copy-start = (f32[2,16,256]{2,1,0:T(8,128)S(1)}, f32[2,16,256]{2,1,0:T(8,128)}, u32[]{:S(2)}) copy-start(f32[2,16,256]{2,1,0:T(8,128)} %param.6) | copy-start | bytes 98308
  2.9 14.8 %all-to-all-start = ((bf16[4,4,7,12,256]{4,1,3,2,0:T(4,128)(2,1)}), bf16[4,4,7,12,256]{4,1,3,2,0:T(4,128)(2,1)S(1)}, u32[]{:S(2)}, u32[]{:S(2)}) async-start(bf16[4,4,7,12,256]{4,1,3,2,0:T(4,128)(2,1)} %pad_maximum_fusion), calls=%async_computation | async-start | bytes 1376256 | tf_op jit(solution)/shard_map/all_to_all | solution.py:46
  20.5 5.8 %copy-start.2 = (bf16[2,256,256]{2,1,0:T(8,128)(2,1)S(1)}, bf16[2,256,256]{2,1,0:T(8,128)(2,1)}, u32[]{:S(2)}) copy-start(bf16[2,256,256]{2,1,0:T(8,128)(2,1)} %param.7) | copy-start | bytes 786436
  20.8 7.5 %collective-permute-start = (bf16[16,7,2,256]{3,0,2,1:T(8,128)(2,1)S(1)}, bf16[16,7,2,256]{3,0,2,1:T(8,128)(2,1)S(1)}, u32[]{:S(2)}, u32[]{:S(2)}) collective-permute-start(bf16[16,7,2,256]{3,0,2,1:T(8,128)(2,1)S(1)} %get-tuple-element.5), channel_id=1, source_target_pairs={{0,1},{1,2},{2,3},{4,5},{5,6},{6,7},{8,9},{9,10},{10,11},{12,13},{... | collective-permute-start | bytes 344072 | tf_op jit(solution)/shard_map/ppermute | solution.py:50
  25.0 6.7 %collective-permute-start.1 = (bf16[16,7,2,256]{3,0,2,1:T(8,128)(2,1)S(1)}, bf16[16,7,2,256]{3,0,2,1:T(8,128)(2,1)S(1)}, u32[]{:S(2)}, u32[]{:S(2)}) collective-permute-start(bf16[16,7,2,256]{3,0,2,1:T(8,128)(2,1)S(1)} %get-tuple-element.6), channel_id=1, source_target_pairs={{1,0},{2,1},{3,2},{5,4},{6,5},{7,6},{9,8},{10,9},{11,10},{13,12},{... | collective-permute-start | bytes 344072 | tf_op jit(solution)/shard_map/ppermute | solution.py:51
  26.3 5.4 %copy-start.1 = (bf16[2,3,3,256,256]{4,3,2,1,0:T(8,128)(2,1)S(1)}, bf16[2,3,3,256,256]{4,3,2,1,0:T(8,128)(2,1)}, u32[]{:S(2)}) copy-start(bf16[2,3,3,256,256]{4,3,2,1,0:T(8,128)(2,1)} %param.5) | copy-start | bytes 7077892
